TPU v7x, 32 devices: a whole 2x2x4 slice. The times are simulated.
32 devices in a mesh: group: 2 (over x), node: 16 (over z, y, core).
Axes of the slice: x: 2, y: 2, z: 4, core: 2. Of those that a mesh axis runs over, the one named last changes fastest.
Arguments:
- states: bfloat16 [512, 2048], P(('group', 'node')), parts along dimension 0, may hold values from -400 to 400
- norm_gain: float32 [2048], replicated, may hold values from 0.5 to 1.5
- picks: int32 [512, 8], P(('group', 'node')), parts along dimension 0, may hold values from 0 to 15, all different within a row; in each aligned block of 16 rows (0 to 15, 16 to 31, ...) at most 16 rows name the same one
- gate_weights: float32 [512, 8], P(('group', 'node')), parts along dimension 0, may hold values from 0.05 to 1
- w_gate: bfloat16 [16, 2048, 768], P('node'), may hold values from -0.125 to 0.125
- w_up: bfloat16 [16, 2048, 768], P('node'), may hold values from -0.125 to 0.125
- w_down: bfloat16 [16, 768, 2048], P('node'), may hold values from -0.21875 to 0.21875
- queries: bfloat16 [128, 4096], P(('group', 'node')), parts along dimension 0, may hold values from -88 to 88
- keys: bfloat16 [128, 256, 512], P(('group', 'node')), parts along dimension 0, may hold values from -4 to 4
- values: bfloat16 [128, 256, 512], P(('group', 'node')), parts along dimension 0, may hold values from -4 to 4
- incoming_keys: bfloat16 [128, 512], P(('group', 'node')), parts along dimension 0, may hold values from -4 to 4
- incoming_values: bfloat16 [128, 512], P(('group', 'node')), parts along dimension 0, may hold values from -4 to 4
- lengths: int32 [128], P(('group', 'node')), parts along dimension 0, may hold values from 32 to 256, as said below
Outputs:
- moe_output: bfloat16 [512, 2048], P(('group', 'node')), parts along dimension 0
- attention_output: bfloat16 [128, 4096], P(('group', 'node')), parts along dimension 0
There are 2 independent parts, one for each index of `group`. A program takes and returns all parts, laid end to end along the dimension named above; an argument that names none is the same for every part. Nothing has to cross between parts.
Inputs may be any that keep to these rules, and one draw needn't show every extreme that they name: Each token picks 8 different experts; among the 16 tokens of one device no expert is picked by more than 16 tokens, a bound that some block reaches. `lengths`: the first request of each device holds 256 cached tokens.
All inputs are finite; a program needn't handle non-finite values.
Results may differ from a plain program's by a relative error of at most 0.0085.
Values may be sent and summed in bfloat16 or wider, within the bound.
No kernel may reach another device: no remote copies, remote signals or barrier semaphores. Data moves between devices by JAX's collectives and lax.ppermute only.
A program may use at most 64 MiB of HBM per device.

v0:
```python
import math
import jax
import jax.numpy as jnp
from jax import lax
from jax.sharding import PartitionSpec as P

QUERY_HEADS = 32
KEY_VALUE_HEADS = 4
HEAD_WIDTH = 128
TOPK = 8
TOK_DEV = 16


def expert_block(received, w_gate, w_up, w_down):
    peers = lax.axis_size("node")
    local_experts = w_gate.shape[0]
    slot_count = received.shape[1]
    features = received.shape[2]
    grouped = received.reshape(peers, local_experts, slot_count, features)
    gate_part = jnp.einsum("nesd,edf->nesf", grouped, w_gate, preferred_element_type=jnp.float32)
    up_part = jnp.einsum("nesd,edf->nesf", grouped, w_up, preferred_element_type=jnp.float32)
    inner = (jax.nn.silu(gate_part) * up_part).astype(jnp.bfloat16)
    produced = jnp.einsum(
        "nesf,efd->nesd", inner, w_down, preferred_element_type=jnp.float32
    ).astype(jnp.bfloat16)
    return produced.reshape(peers * local_experts, slot_count, features)


def route_block(normed, picks, gate_weights, w_gate, w_up, w_down, capacity):
    rows_here = picks.shape[0]
    picks_here = picks.shape[1]
    experts_all = w_gate.shape[0] * lax.axis_size("node")
    features = normed.shape[1]
    flattened = picks.reshape(-1)
    expert_ids = jnp.arange(experts_all, dtype=jnp.int32)
    onehot = (flattened[:, None] == expert_ids[None, :]).astype(jnp.int32)
    earlier = jnp.cumsum(onehot, axis=0) - onehot
    slot_of = jnp.sum(earlier * onehot, axis=1)
    target = flattened * capacity + slot_of
    layout = jnp.arange(experts_all * capacity, dtype=jnp.int32)
    placed = jnp.sum(
        (layout[:, None, None] == target.reshape(rows_here, picks_here)[None, :, :]).astype(
            jnp.int32
        ),
        axis=2,
    )
    outgoing = jnp.dot(placed.astype(jnp.bfloat16), normed, preferred_element_type=jnp.float32)
    outgoing = outgoing.astype(jnp.bfloat16).reshape(experts_all, capacity, features)
    produced = expert_block(
        lax.all_to_all(outgoing, "node", split_axis=0, concat_axis=0, tiled=True),
        w_gate,
        w_up,
        w_down,
    )
    returned = lax.all_to_all(produced, "node", split_axis=0, concat_axis=0, tiled=True)
    gathered = jnp.take(returned.reshape(experts_all * capacity, features), target, axis=0)
    gathered = gathered.reshape(rows_here, picks_here, features)
    shares = gate_weights / jnp.sum(gate_weights, axis=1, keepdims=True)
    return jnp.einsum("tk,tkd->td", shares, gathered.astype(jnp.float32)).astype(jnp.bfloat16)


def dense_block(normed, picks, gate_weights, w_gate, w_up, w_down):
    local_experts = w_gate.shape[0]
    node_index = lax.axis_index("node")
    experts_all = local_experts * lax.axis_size("node")
    shares = gate_weights / jnp.sum(gate_weights, axis=1, keepdims=True)
    expert_ids = jnp.arange(experts_all, dtype=jnp.int32)
    chosen = picks[:, :, None] == expert_ids[None, None, :]
    dense_shares = jnp.sum(jnp.where(chosen, shares[:, :, None], 0.0), axis=1)
    every_row = lax.all_gather(normed, "node", axis=0, tiled=True)
    every_share = lax.all_gather(dense_shares, "node", axis=0, tiled=True)
    own_shares = lax.dynamic_slice_in_dim(
        every_share, node_index * local_experts, local_experts, axis=1
    )
    summed = None
    for expert in range(local_experts):
        gate_part = jnp.dot(every_row, w_gate[expert], preferred_element_type=jnp.float32)
        up_part = jnp.dot(every_row, w_up[expert], preferred_element_type=jnp.float32)
        inner = (jax.nn.silu(gate_part) * up_part).astype(jnp.bfloat16)
        produced = jnp.dot(inner, w_down[expert], preferred_element_type=jnp.float32).astype(
            jnp.bfloat16
        )
        column = own_shares[:, expert : expert + 1]
        weighted = jnp.where(column != 0.0, column * produced.astype(jnp.float32), 0.0)
        summed = weighted if summed is None else summed + weighted
    total = lax.psum_scatter(summed, "node", scatter_dimension=0, tiled=True)
    return total.astype(jnp.bfloat16)


def attend(queries, keys, values, incoming_keys, incoming_values, lengths):
    request_rows = queries.shape[0]
    valid_length = keys.shape[1]
    query_groups = QUERY_HEADS // KEY_VALUE_HEADS
    score_scale = 1.0 / math.sqrt(HEAD_WIDTH)
    query_rows = queries.reshape(request_rows, KEY_VALUE_HEADS, query_groups, HEAD_WIDTH)
    stored_keys = keys.reshape(request_rows, valid_length, KEY_VALUE_HEADS, HEAD_WIDTH)
    stored_values = values.reshape(request_rows, valid_length, KEY_VALUE_HEADS, HEAD_WIDTH)
    scores = (
        jnp.einsum("rkgd,rlkd->rkgl", query_rows, stored_keys, preferred_element_type=jnp.float32)
        * score_scale
    )
    new_token_scores = (
        jnp.einsum(
            "behw,bew->beh",
            query_rows,
            incoming_keys.reshape(request_rows, KEY_VALUE_HEADS, HEAD_WIDTH),
            preferred_element_type=jnp.float32,
        )
        * score_scale
    )
    present = (jnp.arange(valid_length, dtype=jnp.int32)[None, :] < lengths[:, None])[
        :, None, None, :
    ]
    masked = jnp.where(present, scores, -1e30)
    highest = jnp.maximum(jnp.max(masked, axis=3), new_token_scores)
    raised = jnp.where(present, jnp.exp(masked - highest[..., None]), 0.0)
    fresh_raised = jnp.exp(new_token_scores - highest)
    denominator = jnp.sum(raised, axis=3) + fresh_raised
    probs = (raised / denominator[..., None]).astype(jnp.bfloat16)
    new_token_probability = (fresh_raised / denominator).astype(jnp.bfloat16)
    blended_output = jnp.einsum(
        "rkgl,rlkd->rkgd", probs, stored_values, preferred_element_type=jnp.float32
    )
    blended_output = blended_output + new_token_probability.astype(jnp.float32)[
        ..., None
    ] * incoming_values.reshape(request_rows, KEY_VALUE_HEADS, 1, HEAD_WIDTH).astype(jnp.float32)
    return blended_output.reshape(request_rows, QUERY_HEADS * HEAD_WIDTH).astype(jnp.bfloat16)


def on_device(
    states,
    norm_gain,
    picks,
    gate_weights,
    w_gate,
    w_up,
    w_down,
    queries,
    keys,
    values,
    incoming_keys,
    incoming_values,
    lengths,
):
    widened = states.astype(jnp.float32)
    meansq = jnp.mean(widened * widened, axis=1, keepdims=True) + 1e-06
    normed = (widened / jnp.sqrt(meansq) * norm_gain[None, :]).astype(jnp.bfloat16)
    experts_all = w_gate.shape[0] * lax.axis_size("node")
    capacity = min(TOK_DEV, max(2, 2 * TOK_DEV * TOPK // experts_all))
    gathered_rows = normed.shape[0] * lax.axis_size("node")
    if gathered_rows <= experts_all * capacity:
        moe_output = dense_block(normed, picks, gate_weights, w_gate, w_up, w_down)
    else:
        moe_output = route_block(normed, picks, gate_weights, w_gate, w_up, w_down, capacity)
    attention_output = attend(queries, keys, values, incoming_keys, incoming_values, lengths)
    return (moe_output, attention_output)


def solution(mesh):
    in_specs = (
        P(("group", "node"), None),
        P(),
        P(("group", "node"), None),
        P(("group", "node"), None),
        P("node", None, None),
        P("node", None, None),
        P("node", None, None),
        P(("group", "node"), None),
        P(("group", "node"), None, None),
        P(("group", "node"), None, None),
        P(("group", "node"), None),
        P(("group", "node"), None),
        P(("group", "node")),
    )
    out_specs = (P(("group", "node"), None), P(("group", "node"), None))
    return jax.shard_map(
        on_device, mesh=mesh, in_specs=in_specs, out_specs=out_specs, check_vma=False
    )
```

profile of v0, /device:TPU:0, one launch (start us, length us, event | category | flops | bytes accessed | tf_op | source)
XLA Modules:
  0.0 130.5 jit_solution(14957401448452033666)
XLA Ops:
  7.2 0.0 all-gather.2.cloned.1.call-start
  7.2 1.1 fusion.38
  8.4 1.6 %fusion.40 = bf16[16,2048]{1,0:T(8,128)(2,1)} fusion(bf16[16,2048]{1,0:T(8,128)(2,1)} %param.13, f32[2048]{0:T(1024)} %param.14, f32[16]{0:T(128)S(1)} %add_sqrt_fusion), kind=kLoop, calls=%fused_computation.30 | loop fusion | flops 131072 | bytes 139328 | tf_op jit(solution)/shard_map/convert_element_type | solution.py:147
  9.9 0.0 all-gather.2.cloned.1.call-update
  9.9 0.0 reduce-scatter.2.cloned.1.call-start
  10.0 0.7 reduce_sum.36
  10.7 0.7 broadcast_divide_fusion
  11.4 0.1 copy.28
  11.5 0.8 copy.27
  12.2 0.1 select_reduce_fusion
  12.3 23.5 %all_gather.6 = f32[256,16]{1,0:T(8,128)S(1)} all-gather(f32[16,16]{1,0:T(8,128)S(1)} %select_reduce_fusion), channel_id=1, replica_groups=mesh['group'=2,'node'=16] {'node'}, dimensions={0}, use_global_device_ids=true | all-gather | bytes 17408 | tf_op jit(solution)/shard_map/all_gather | solution.py:71
  35.9 0.2 dynamic-slice_reduce_fusion
  36.0 0.2 compare_reduce_fusion
  36.2 15.2 %all-gather.2.cloned.1.call-done = bf16[256,2048]{1,0:T(8,128)(2,1)} async-done(((bf16[16,2048]{1,0:T(8,128)(2,1)}), bf16[256,2048]{1,0:T(8,128)(2,1)}) %all-gather.2.cloned.1.call-update) | async-done | bytes 1048592 | tf_op jit(solution)/shard_map/all_gather | solution.py:70
  51.5 4.1 %fusion.4 = f32[256,768]{1,0:T(8,128)} fusion(bf16[256,2048]{1,0:T(8,128)(2,1)} %all-gather.2.cloned.1.call-done, bf16[1,2048,768]{2,1,0:T(8,128)(2,1)} %param.17), kind=kOutput, calls=%fused_computation.4 | convolution fusion | flops 805306368 | bytes 4980736 | tf_op jit(solution)/shard_map/dot_general | solution.py:77
  55.6 5.9 %fusion.15 = f32[256,2048]{1,0:T(8,128)} fusion(bf16[1,768,2048]{2,1,0:T(8,128)(2,1)S(1)} %copy-done, f32[256]{0:T(256)S(1)} %dynamic-slice_reduce_fusion, pred[256]{0:T(512)(128)(4,1)S(1)} %compare_reduce_fusion, bf16[256,2048]{1,0:T(8,128)(2,1)} %all-gather.2.cloned.1.call-done, bf16[1,2048,768]{2,1,0:T(8,128)(2,1)} %param.18, f32[256,768]{1,0:T(8,128)} %fusion.4), kind=kOutput, calls=%fused_computation.9 | convolution fusion | flops 1613889536 | bytes 10224896 | tf_op jit(solution)/shard_map/dot_general | solution.py:80
  61.5 0.1 iota_compare_fusion.1
  61.6 0.1 fusion.46
  61.8 1.7 %fusion.55 = (f32[4,4,8]{2,1,0:T(4,128)S(1)}, f32[4,4,8,256]{3,2,1,0:T(8,128)S(1)}) fusion(bf16[1,4,32,128]{3,1,2,0:T(4,128)(2,1)S(1)} %bitcast.60, pred[4,256]{1,0:T(4,128)(4,1)S(1)} %iota_compare_fusion.1, bf16[4,256,512]{2,1,0:T(8,128)(2,1)} %param.21), kind=kOutput, calls=%fused_computation.58 | convolution fusion | flops 8486784 | bytes 1213952 | tf_op jit(solution)/shard_map/rkgd,rlkd->rkgl/dot_general | solution.py:99
  63.5 0.2 fusion.41
  63.7 1.5 %fusion.26 = bf16[1,4,32,128]{3,2,1,0:T(8,128)(2,1)S(1)} fusion(f32[4,4,8,256]{3,2,1,0:T(8,128)S(1)} %get-tuple-element.5, f32[4,4,8]{2,1,0:T(4,128)S(1)} %get-tuple-element.3, f32[4,4,8]{2,1,0:T(4,128)S(1)} %multiply_maximum_fusion, pred[4,256]{1,0:T(4,128)(4,1)S(1)} %iota_compare_fusion.1, f32[4,4,128]{2,1,0:T(4,128)S(1)} %reshape.64, ...), kind=kOutput, calls=%fused_computation.16 | convolution fusion | flops 8568832 | bytes 1223168 | tf_op jit(solution)/shard_map/rkgl,rlkd->rkgd/dot_general | solution.py:121
  65.2 0.6 copy.58
  65.9 56.2 %reduce-scatter.2.cloned.1.call-done = f32[16,2048]{1,0:T(8,128)} async-done(((f32[256,2048]{1,0:T(8,128)}), f32[16,2048]{1,0:T(8,128)}) %reduce-scatter.2.cloned.1.call-update) | async-done | bytes 131088 | tf_op jit(solution)/shard_map/reduce_scatter | solution.py:86
  122.1 1.5 %convert_element_type.49 = bf16[16,2048]{1,0:T(8,128)(2,1)} convert(f32[16,2048]{1,0:T(8,128)} %reduce-scatter.2.cloned.1.call-done) | non-fusion elementwise | flops 32768 | bytes 196608 | tf_op jit(solution)/shard_map/convert_element_type | solution.py:87
  (16 shorter events, 0.1 us)
Async XLA Ops:
  7.2 48.4 %copy-start = (bf16[1,768,2048]{2,1,0:T(8,128)(2,1)S(1)}, bf16[1,768,2048]{2,1,0:T(8,128)(2,1)}, u32[]{:S(2)}) copy-start(bf16[1,768,2048]{2,1,0:T(8,128)(2,1)} %param.19) | copy-start | bytes 9437188
  7.2 44.3 %all-gather.2.cloned.1.call-start = ((), (), s32[]{:S(2)}) async-start(), calls=%async_computation.1 | async-start | bytes 1114112 | tf_op jit(solution)/shard_map/all_gather | solution.py:70
  9.9 112.1 %reduce-scatter.2.cloned.1.call-start = ((), (), s32[]{:S(2)}) async-start(), calls=%async_computation.2 | async-start | bytes 2228224 | tf_op jit(solution)/shard_map/reduce_scatter | solution.py:86
  55.5 6.0 %copy-start.2 = (bf16[4,512]{1,0:T(4,128)(2,1)S(1)}, bf16[4,512]{1,0:T(4,128)(2,1)}, u32[]{:S(2)}) copy-start(bf16[4,512]{1,0:T(4,128)(2,1)} %param.23) | copy-start | bytes 12292
  55.5 6.0 %copy-start.3 = (bf16[4,512]{1,0:T(4,128)(2,1)S(1)}, bf16[4,512]{1,0:T(4,128)(2,1)}, u32[]{:S(2)}) copy-start(bf16[4,512]{1,0:T(4,128)(2,1)} %param.24) | copy-start | bytes 12292
  55.5 6.0 %copy-start.4 = (s32[4]{0:T(128)S(1)}, s32[4]{0:T(128)}, u32[]{:S(2)}) copy-start(s32[4]{0:T(128)} %param.25) | copy-start | bytes 52
  55.5 6.1 %copy-start.1 = (bf16[4,4096]{1,0:T(4,128)(2,1)S(1)}, bf16[4,4096]{1,0:T(4,128)(2,1)}, u32[]{:S(2)}) copy-start(bf16[4,4096]{1,0:T(4,128)(2,1)} %param.20) | copy-start | bytes 98308
Sparse Core Ops, SparseCore 0:
  10.7 40.6 all-gather.1
  61.6 60.4 reduce-scatter.1
where the time goes:
time: 131 us; the launch traced here: 130 us
  waiting for transfers between devices  71.5 us (55%)
  blocking collectives  23.5 us (18%)
  between operations  14.1 us (11%)
  matrix products  13.3 us (10%)
  other arithmetic  6.23 us (5%)
  local copies, waits for them, and re-layouts  1.71 us (1%)
    reduce_scatter x1, waiting for transfers between devices, dense_block(): total = lax.psum_scatter(summed, 'node', scatter_dimension=0, tiled=True)  56.2 us
    all_gather x1, blocking collectives, dense_block(): every_share = lax.all_gather(dense_shares, 'node', axis=0, tiled=True)  23.5 us
    all_gather x1, waiting for transfers between devices, dense_block(): every_row = lax.all_gather(normed, 'node', axis=0, tiled=True)  15.2 us
    dot_general x1, matrix products, dense_block(): jnp.dot(inner, w_down[expert], preferred_element_type=jnp.float32)  5.91 us
    dot_general x1, matrix products, dense_block(): jnp.dot(every_row, w_gate[expert], preferred_element_type=jnp.float32)  4.07 us
  transfers between devices with their start and end apart: 2, of which 2 were waited for; matrix products, arithmetic and copies ran while one was open for 5% of the time, Pallas kernels for 0%

commit v1 on v0

--- a/solution.py
+++ b/solution.py
@@ -67,8 +67,11 @@
     expert_ids = jnp.arange(experts_all, dtype=jnp.int32)
     chosen = picks[:, :, None] == expert_ids[None, None, :]
     dense_shares = jnp.sum(jnp.where(chosen, shares[:, :, None], 0.0), axis=1)
-    every_row = lax.all_gather(normed, "node", axis=0, tiled=True)
-    every_share = lax.all_gather(dense_shares, "node", axis=0, tiled=True)
+    every_row, every_share = jnp.split(
+        lax.all_gather(jnp.concatenate([normed, dense_shares], axis=1), "node", axis=0, tiled=True),
+        [normed.shape[1]],
+        axis=1,
+    )
     own_shares = lax.dynamic_slice_in_dim(
         every_share, node_index * local_experts, local_experts, axis=1
     )

time: 131 us -> 138 us (1.053)
  waiting for transfers between devices: 71.5 us -> 101 us
  blocking collectives: 23.5 us -> 0 us
    all_gather x1, waiting for transfers between devices: 15.2 us -> 44.6 us  [dense_block(): lax.all_gather(jnp.concatenate([normed, dense_shares], axis=1), 'node', a...]
    all_gather x1 -> x0, blocking collectives: 23.5 us -> none  [dense_block(): every_share = lax.all_gather(dense_shares, 'node', axis=0, tiled=True)]
  transfers between devices with their start and end apart: 2 -> 2, of which waited for: 2 -> 2; matrix products, arithmetic and copies ran while one was open for 5% -> 3% of each run, Pallas kernels for 0% -> 0%
where the time goes in v1:
time: 138 us
  waiting for transfers between devices  101 us (73%)
  between operations  14.1 us (10%)
  matrix products  13.9 us (10%)
  other arithmetic  6.32 us (5%)
  local copies, waits for them, and re-layouts  2.62 us (2%)
    reduce_scatter x1, waiting for transfers between devices, dense_block(): total = lax.psum_scatter(summed, 'node', scatter_dimension=0, tiled=True)  56.3 us
    all_gather x1, waiting for transfers between devices, dense_block(): lax.all_gather(jnp.concatenate([normed, dense_shares], axis=1), 'node', a...  44.6 us
    dot_general x1, matrix products, dense_block(): jnp.dot(inner, w_down[expert], preferred_element_type=jnp.float32)  6.18 us
    dot_general x1, matrix products, dense_block(): jnp.dot(every_row, w_gate[expert], preferred_element_type=jnp.float32)  4.4 us
  transfers between devices with their start and end apart: 2, of which 2 were waited for; matrix products, arithmetic and copies ran while one was open for 3% of the time, Pallas kernels for 0%

profile of v1, /device:TPU:0, one launch (start us, length us, event | category | flops | bytes accessed | tf_op | source)
XLA Modules:
  0.0 138.0 jit_solution(844680667461639819)
XLA Ops:
  7.2 0.0 all-gather.2.cloned.1.call-start
  7.2 0.9 reduce_sum.37
  8.1 0.7 broadcast_divide_fusion
  8.8 0.1 copy.24
  8.9 0.8 copy.23
  9.7 1.0 fusion.42
  10.6 0.1 select_reduce_fusion
  10.8 0.9 fusion.46
  11.7 0.7 pad_maximum_fusion
  12.4 0.0 reduce-scatter.2.cloned.1.call-start
  12.4 44.6 %all-gather.2.cloned.1.call-done = f32[256,2064]{1,0:T(8,128)} async-done(((f32[16,2064]{1,0:T(8,128)}), f32[256,2064]{1,0:T(8,128)}) %all-gather.2.cloned.1.call-update) | async-done | bytes 2113552 | tf_op jit(solution)/shard_map/all_gather | solution.py:71
  57.0 0.9 split.8
  58.0 0.2 dynamic-slice_reduce_fusion
  58.1 0.2 compare_reduce_fusion
  58.3 4.4 %fusion.4 = f32[256,768]{1,0:T(8,128)} fusion(bf16[1,2048,768]{2,1,0:T(8,128)(2,1)} %param.17, f32[256,2064]{1,0:T(8,128)} %all-gather.2.cloned.1.call-done), kind=kOutput, calls=%fused_computation.4 | convolution fusion | flops 805306368 | bytes 4980736 | tf_op jit(solution)/shard_map/dot_general | solution.py:80
  62.8 6.2 %fusion.15 = f32[256,2048]{1,0:T(8,128)} fusion(bf16[1,768,2048]{2,1,0:T(8,128)(2,1)S(1)} %copy-done, f32[256]{0:T(256)S(1)} %dynamic-slice_reduce_fusion, pred[256]{0:T(512)(128)(4,1)S(1)} %compare_reduce_fusion, bf16[1,2048,768]{2,1,0:T(8,128)(2,1)} %param.18, f32[256,2064]{1,0:T(8,128)} %all-gather.2.cloned.1.call-done, f32[256,768]{1,0:T(8,128)} %fusion.4), kind=kOutput, calls=%fused_computation.9 | convolution fusion | flops 1613889536 | bytes 10224896 | tf_op jit(solution)/shard_map/dot_general | solution.py:83
  69.0 0.1 iota_compare_fusion.1
  69.1 0.1 fusion.51
  69.2 1.7 %fusion.60 = (f32[4,4,8]{2,1,0:T(4,128)S(1)}, f32[4,4,8,256]{3,2,1,0:T(8,128)S(1)}) fusion(bf16[1,4,32,128]{3,1,2,0:T(4,128)(2,1)S(1)} %bitcast.58, pred[4,256]{1,0:T(4,128)(4,1)S(1)} %iota_compare_fusion.1, bf16[4,256,512]{2,1,0:T(8,128)(2,1)} %param.21), kind=kOutput, calls=%fused_computation.58 | convolution fusion | flops 8486784 | bytes 1213952 | tf_op jit(solution)/shard_map/rkgd,rlkd->rkgl/dot_general | solution.py:102
  70.9 0.2 fusion.45
  71.2 1.5 %fusion.32 = bf16[1,4,32,128]{3,2,1,0:T(8,128)(2,1)S(1)} fusion(f32[4,4,8,256]{3,2,1,0:T(8,128)S(1)} %get-tuple-element.5, f32[4,4,8]{2,1,0:T(4,128)S(1)} %get-tuple-element.3, f32[4,4,8]{2,1,0:T(4,128)S(1)} %multiply_maximum_fusion, pred[4,256]{1,0:T(4,128)(4,1)S(1)} %iota_compare_fusion.1, f32[4,4,128]{2,1,0:T(4,128)S(1)} %reshape.64, ...), kind=kOutput, calls=%fused_computation.18 | convolution fusion | flops 8568832 | bytes 1223168 | tf_op jit(solution)/shard_map/rkgl,rlkd->rkgd/dot_general | solution.py:124
  72.7 0.6 copy.54
  73.3 56.3 %reduce-scatter.2.cloned.1.call-done = f32[16,2048]{1,0:T(8,128)} async-done(((f32[256,2048]{1,0:T(8,128)}), f32[16,2048]{1,0:T(8,128)}) %reduce-scatter.2.cloned.1.call-update) | async-done | bytes 131088 | tf_op jit(solution)/shard_map/reduce_scatter | solution.py:89
  129.6 1.5 %convert_element_type.53 = bf16[16,2048]{1,0:T(8,128)(2,1)} convert(f32[16,2048]{1,0:T(8,128)} %reduce-scatter.2.cloned.1.call-done) | non-fusion elementwise | flops 32768 | bytes 196608 | tf_op jit(solution)/shard_map/convert_element_type | solution.py:90
  (17 shorter events, 0.1 us)
Async XLA Ops:
  7.2 55.6 %copy-start = (bf16[1,768,2048]{2,1,0:T(8,128)(2,1)S(1)}, bf16[1,768,2048]{2,1,0:T(8,128)(2,1)}, u32[]{:S(2)}) copy-start(bf16[1,768,2048]{2,1,0:T(8,128)(2,1)} %param.19) | copy-start | bytes 9437188
  7.2 49.9 %all-gather.2.cloned.1.call-start = ((), (), s32[]{:S(2)}) async-start(), calls=%async_computation.1 | async-start | bytes 2367488 | tf_op jit(solution)/shard_map/all_gather | solution.py:71
  12.4 117.2 %reduce-scatter.2.cloned.1.call-start = ((), (), s32[]{:S(2)}) async-start(), calls=%async_computation.2 | async-start | bytes 2228224 | tf_op jit(solution)/shard_map/reduce_scatter | solution.py:89
  62.7 6.2 %copy-start.2 = (bf16[4,512]{1,0:T(4,128)(2,1)S(1)}, bf16[4,512]{1,0:T(4,128)(2,1)}, u32[]{:S(2)}) copy-start(bf16[4,512]{1,0:T(4,128)(2,1)} %param.23) | copy-start | bytes 12292
  62.7 6.3 %copy-start.3 = (bf16[4,512]{1,0:T(4,128)(2,1)S(1)}, bf16[4,512]{1,0:T(4,128)(2,1)}, u32[]{:S(2)}) copy-start(bf16[4,512]{1,0:T(4,128)(2,1)} %param.24) | copy-start | bytes 12292
  62.7 6.3 %copy-start.4 = (s32[4]{0:T(128)S(1)}, s32[4]{0:T(128)}, u32[]{:S(2)}) copy-start(s32[4]{0:T(128)} %param.25) | copy-start | bytes 52
  62.7 6.4 %copy-start.1 = (bf16[4,4096]{1,0:T(4,128)(2,1)S(1)}, bf16[4,4096]{1,0:T(4,128)(2,1)}, u32[]{:S(2)}) copy-start(bf16[4,4096]{1,0:T(4,128)(2,1)} %param.20) | copy-start | bytes 98308
Sparse Core Ops, SparseCore 0:
  12.5 44.4 all-gather.1
  69.1 60.4 reduce-scatter.1
